TPU v7x, 512 devices: a whole 4x8x8 slice. The times are simulated.
512 devices in a mesh: slab: 64 (over z, x, core), obs: 8 (over y).
Axes of the slice: x: 4, y: 8, z: 8, core: 2. Of those that a mesh axis runs over, the one named last changes fastest.
Arguments:
- background_members: float32 [64, 1048576], P('slab', 'obs'), may hold values from -6 to 6
- measurement_jitter: bfloat16 [64, 8, 65536], P(None, 'obs', 'slab'), may hold values from -5 to 5
- measurement_readings: float32 [8, 65536], P('obs', 'slab'), may hold values from -8 to 8
- measurement_noise_spread: float32 [8, 65536], P('obs', 'slab'), may hold values from 0.2 to 2
- measurement_grid_location: int32 [8, 65536], P('obs', 'slab'), may hold values from 0 to 2047
- active_tallies: int32 [8, 64], P('obs', 'slab'), may hold values from 128 to 1024, as said below
- coupling_listing: int32 [8, 2048, 8], P('obs', 'slab'), may hold values from 0 to 63, as said below
- taper_factors: float32 [8, 2048, 8], P('obs', 'slab'), may hold values from 0.1 to 1
Outputs:
- analysis: float32 [64, 1048576], P('slab', 'obs')
Inputs may be any that keep to these rules, and one draw needn't show every extreme that they name: `active_tallies`: some region of some group holds 1024 live observations; slots beyond a region's count are padding. `coupling_listing`: the 8 observation blocks listed for a state block are distinct.
All inputs are finite; a program needn't handle non-finite values.
Results may differ from a plain program's by a relative error of at most 0.0063.
Values may be sent and summed in bfloat16 or wider, within the bound.
No kernel may reach another device: no remote copies, remote signals or barrier semaphores. Data moves between devices by JAX's collectives and lax.ppermute only.
A program may use at most 64 MiB of HBM per device.

v0:
```python
import math
import jax
import jax.numpy as jnp
from jax import lax
from jax.sharding import PartitionSpec as P

OB = 128
highest = lax.Precision.HIGHEST


def compute_increment(
    tile_work,
    measurement_jitter,
    measurement_readings,
    measurement_noise_spread,
    measurement_grid_location,
    active_tallies,
    coupling_listing,
    taper_factors,
):
    members = tile_work.shape[0]
    points = tile_work.shape[1]
    blocks = coupling_listing.shape[1]
    block_width = points // blocks
    deviation = tile_work - jnp.mean(tile_work, axis=0, keepdims=True)
    positions = measurement_grid_location[0]
    obs_count = positions.shape[0]
    prior_value = jnp.take(tile_work, positions, axis=1)
    prior_shift = prior_value - jnp.mean(prior_value, axis=0, keepdims=True)
    spread = jnp.sum(prior_shift * prior_shift, axis=0, keepdims=True) / (members - 1)
    usable = jnp.arange(obs_count, dtype=jnp.int32)[None, :] < active_tallies[0, 0]
    innovation = (
        measurement_readings + measurement_jitter[:, 0, :].astype(jnp.float32) - prior_value
    ) / (spread + measurement_noise_spread)
    gain_input = jnp.where(usable, innovation, jnp.float32(0.0)).astype(jnp.bfloat16)
    prior_low = prior_shift.astype(jnp.bfloat16)
    block_links = coupling_listing[0]
    factor = taper_factors[0] / (members - 1)
    gathered = (
        lax.all_gather(prior_low, "obs", axis=1, tiled=True),
        lax.all_gather(gain_input, "obs", axis=1, tiled=True),
    )
    all_prior = gathered[0].reshape(members, -1, OB)
    all_gain = gathered[1].reshape(members, -1, OB)
    group_size = math.gcd(blocks, 8)
    group_count = blocks // group_size

    def one_group(group_index, running):
        first_block = group_index * group_size
        local_dev = lax.dynamic_slice_in_dim(
            deviation, first_block * block_width, group_size * block_width, 1
        )
        local_dev = local_dev.reshape(members, group_size, block_width)
        chosen = lax.dynamic_slice_in_dim(block_links, first_block, group_size, 0)
        scales = lax.dynamic_slice_in_dim(factor, first_block, group_size, 0)
        picked_prior = jnp.take(all_prior, chosen, axis=1).astype(jnp.float32)
        picked_gain = jnp.take(all_gain, chosen, axis=1).astype(jnp.float32)
        covariance = jnp.einsum("mgp,mglo->glpo", local_dev, picked_prior, precision=highest)
        update = jnp.einsum("glpo,mglo,gl->mgp", covariance, picked_gain, scales, precision=highest)
        update = update.reshape(members, group_size * block_width)
        return lax.dynamic_update_slice_in_dim(running, update, first_block * block_width, 1)

    increment = lax.fori_loop(0, group_count, one_group, jnp.zeros_like(deviation))
    return increment.astype(jnp.bfloat16)


def local(
    background_members,
    measurement_jitter,
    measurement_readings,
    measurement_noise_spread,
    measurement_grid_location,
    active_tallies,
    coupling_listing,
    taper_factors,
):
    grid_segment_piece = lax.all_to_all(
        background_members, "slab", split_axis=1, concat_axis=0, tiled=True
    )
    tile_work = lax.optimization_barrier(grid_segment_piece.astype(jnp.bfloat16)).astype(
        jnp.float32
    )
    reduced_correction = compute_increment(
        tile_work,
        measurement_jitter,
        measurement_readings,
        measurement_noise_spread,
        measurement_grid_location,
        active_tallies,
        coupling_listing,
        taper_factors,
    )
    analysis = grid_segment_piece + lax.optimization_barrier(reduced_correction).astype(jnp.float32)
    return lax.all_to_all(analysis, "slab", split_axis=0, concat_axis=1, tiled=True)


def solution(mesh):
    return jax.shard_map(
        local,
        mesh=mesh,
        in_specs=(
            P("slab", "obs"),
            P(None, "obs", "slab"),
            P("obs", "slab"),
            P("obs", "slab"),
            P("obs", "slab"),
            P("obs", "slab"),
            P("obs", "slab", None),
            P("obs", "slab", None),
        ),
        out_specs=P("slab", "obs"),
        check_vma=False,
    )
```

profile of v0, /device:TPU:1, one launch (start us, length us, event | category | flops | bytes accessed | tf_op | source)
XLA Modules:
  0.0 229.1 jit_solution(7997305621396136883)
XLA Ops:
  6.5 14.8 %all-to-all-start = ((f32[1,64,2048]{2,0,1:T(1,128)}), f32[1,64,2048]{2,0,1:T(1,128)S(1)}, u32[]{:S(2)}, u32[]{:S(2)}) async-start(f32[1,64,2048]{2,0,1:T(1,128)} %bitcast.93), calls=%async_computation | async-start | bytes 1048576 | tf_op jit(solution)/shard_map/all_to_all | solution.py:77
  22.1 1.1 copy.33
  23.1 0.7 iota_compare_fusion
  23.8 0.7 compare_select_fusion.1
  24.5 14.5 %all-to-all-done = f32[1,64,2048]{2,0,1:T(1,128)S(1)} async-done(((f32[1,64,2048]{2,0,1:T(1,128)}), f32[1,64,2048]{2,0,1:T(1,128)S(1)}, u32[]{:S(2)}, u32[]{:S(2)}) %all-to-all-start) | async-done | bytes 524320 | tf_op jit(solution)/shard_map/all_to_all | solution.py:77
  39.1 0.2 copy.51
  39.2 0.7 copy-done
  39.9 0.2 copy.34
  40.1 2.8 %gather_fusion.2 = f32[1024,64]{1,0:T(8,128)S(1)} fusion(f32[64,2048]{0,1:T(8,128)S(1)} %copy.34, s32[1024]{0:T(1024)S(1)} %broadcast_clamp_fusion), kind=kCustom, calls=%fused_computation.2 | custom fusion | bytes 528384 | tf_op jit(solution)/shard_map/jit(_take)/gather | solution.py:28
  43.0 0.4 select_reduce_fusion
  43.3 1.0 fusion.18
  44.4 1.6 fusion.17
  46.1 0.7 all-gather.5.cloned.1.call-update
  46.8 0.1 copy.32
  47.0 0.8 broadcast_subtract_fusion
  47.8 33.9 %all-gather.3.cloned.1.call-done = bf16[64,8192]{0,1:T(8,128)(2,1)} async-done(((bf16[64,1024]{0,1:T(8,128)(2,1)}), bf16[64,8192]{0,1:T(8,128)(2,1)}) %all-gather.3.cloned.1.call-update) | async-done | bytes 1048592 | tf_op jit(solution)/shard_map/all_gather | solution.py:41
  81.7 2.7 %copy.35 = bf16[64,64,128]{2,0,1:T(8,128)(2,1)} copy(bf16[64,64,128]{0,2,1:T(8,128)(2,1)} %bitcast.90) | data formatting | bytes 2097152 | tf_op jit(solution)/shard_map/while | solution.py:63
  84.4 41.5 %all-gather.5.cloned.1.call-done = bf16[64,8192]{0,1:T(8,128)(2,1)} async-done(((bf16[64,1024]{0,1:T(8,128)(2,1)}), bf16[64,8192]{0,1:T(8,128)(2,1)}) %all-gather.5.cloned.1.call-update) | async-done | bytes 1048592 | tf_op jit(solution)/shard_map/all_gather | solution.py:40
  126.0 2.7 %copy.36 = bf16[64,64,128]{2,0,1:T(8,128)(2,1)} copy(bf16[64,64,128]{0,2,1:T(8,128)(2,1)} %bitcast.91) | data formatting | bytes 2097152 | tf_op jit(solution)/shard_map/while | solution.py:63
  128.7 58.3 %while.15 = (s32[]{:T(128)}, bf16[64,2048]{1,0:T(8,128)(2,1)S(1)}, s32[32,8]{1,0:T(8,128)S(1)}, bf16[64,64,128]{2,0,1:T(8,128)(2,1)}, bf16[64,64,128]{2,0,1:T(8,...) while((s32[]{:T(128)}, bf16[64,2048]{1,0:T(8,128)(2,1)S(1)}, ...), condition=%wide.region_4.6_spmd, body=%wide.region_3.5_spmd.sunk | while | flops 809502080 | bytes 13704617 | solution.py:63
  128.7 0.1 reshape.156
  128.8 2.0 gather_fusion
  130.8 0.9 constant_dynamic-slice_fusion.2
  131.7 0.1 copy.58
  131.9 2.4 %fusion.36 = f32[8,8,128,64]{2,3,1,0:T(8,128)} fusion(f32[64,8,64,1]{0,2,3,1:T(8,128)S(1)} %bitcast.85, bf16[8,8,64,128]{3,2,1,0:T(8,128)(2,1)S(1)} %bitcast.83, pred[8,8]{1,0:T(8,128)(4,1)S(1)} %get-tuple-element.277), kind=kOutput, calls=%fused_computation.6.clone.1 | convolution fusion | flops 403177472 | bytes 3276864 | tf_op jit(solution)/shard_map/while/body/eval_jaxpr/mgp,mglo->glpo/dot_general | solution.py:58
  134.2 2.0 gather_fusion.1
  136.2 3.4 %convolution_bitcast_fusion.2 = f32[64,8,8,64]{3,0,2,1:T(8,128)S(1)} fusion(f32[8,8,128,64]{2,3,1,0:T(8,128)} %fusion.36, bf16[8,8,64,128]{3,2,1,0:T(8,128)(2,1)S(1)} %bitcast.84, pred[8,8]{1,0:T(8,128)(4,1)S(1)} %get-tuple-element.277), kind=kOutput, calls=%fused_computation.5.clone.1 | convolution fusion | flops 403177472 | bytes 4194368 | tf_op jit(solution)/shard_map/while/body/eval_jaxpr/glpo,mglo,gl->mgp/dot_general | solution.py:59
  139.8 3.1 %fusion.37 = bf16[8,1,64,64]{3,1,2,0:T(2,128)(2,1)S(1)} fusion(f32[8,8,1,1]{1,2,3,0:T(1,128)S(1)} %copy.57, f32[64,8,8,64]{3,0,2,1:T(8,128)S(1)} %convolution_bitcast_fusion.2), kind=kOutput, calls=%fused_computation.3.clone.1 | convolution fusion | flops 3145728 | bytes 1114368 | tf_op jit(solution)/shard_map/while/body/eval_jaxpr/glpo,mglo,gl->mgp/dot_general | solution.py:59
  142.9 0.2 copy.59
  143.1 0.1 reshape.157
  143.3 0.1 reshape.156
  143.4 2.0 gather_fusion
  145.4 0.9 constant_dynamic-slice_fusion.2
  146.3 0.1 copy.58
  146.4 2.4 %fusion.36 = f32[8,8,128,64]{2,3,1,0:T(8,128)} fusion(f32[64,8,64,1]{0,2,3,1:T(8,128)S(1)} %bitcast.85, bf16[8,8,64,128]{3,2,1,0:T(8,128)(2,1)S(1)} %bitcast.83, pred[8,8]{1,0:T(8,128)(4,1)S(1)} %get-tuple-element.277), kind=kOutput, calls=%fused_computation.6.clone.1 | convolution fusion | flops 403177472 | bytes 3276864 | tf_op jit(solution)/shard_map/while/body/eval_jaxpr/mgp,mglo->glpo/dot_general | solution.py:58
  148.8 2.0 gather_fusion.1
  150.8 3.4 %convolution_bitcast_fusion.2 = f32[64,8,8,64]{3,0,2,1:T(8,128)S(1)} fusion(f32[8,8,128,64]{2,3,1,0:T(8,128)} %fusion.36, bf16[8,8,64,128]{3,2,1,0:T(8,128)(2,1)S(1)} %bitcast.84, pred[8,8]{1,0:T(8,128)(4,1)S(1)} %get-tuple-element.277), kind=kOutput, calls=%fused_computation.5.clone.1 | convolution fusion | flops 403177472 | bytes 4194368 | tf_op jit(solution)/shard_map/while/body/eval_jaxpr/glpo,mglo,gl->mgp/dot_general | solution.py:59
  154.4 3.1 %fusion.37 = bf16[8,1,64,64]{3,1,2,0:T(2,128)(2,1)S(1)} fusion(f32[8,8,1,1]{1,2,3,0:T(1,128)S(1)} %copy.57, f32[64,8,8,64]{3,0,2,1:T(8,128)S(1)} %convolution_bitcast_fusion.2), kind=kOutput, calls=%fused_computation.3.clone.1 | convolution fusion | flops 3145728 | bytes 1114368 | tf_op jit(solution)/shard_map/while/body/eval_jaxpr/glpo,mglo,gl->mgp/dot_general | solution.py:59
  157.5 0.2 copy.59
  157.7 0.1 reshape.157
  157.9 0.1 reshape.156
  158.0 2.0 gather_fusion
  159.9 0.9 constant_dynamic-slice_fusion.2
  160.9 0.1 copy.58
  161.0 2.4 %fusion.36 = f32[8,8,128,64]{2,3,1,0:T(8,128)} fusion(f32[64,8,64,1]{0,2,3,1:T(8,128)S(1)} %bitcast.85, bf16[8,8,64,128]{3,2,1,0:T(8,128)(2,1)S(1)} %bitcast.83, pred[8,8]{1,0:T(8,128)(4,1)S(1)} %get-tuple-element.277), kind=kOutput, calls=%fused_computation.6.clone.1 | convolution fusion | flops 403177472 | bytes 3276864 | tf_op jit(solution)/shard_map/while/body/eval_jaxpr/mgp,mglo->glpo/dot_general | solution.py:58
  163.4 2.0 gather_fusion.1
  165.4 3.4 %convolution_bitcast_fusion.2 = f32[64,8,8,64]{3,0,2,1:T(8,128)S(1)} fusion(f32[8,8,128,64]{2,3,1,0:T(8,128)} %fusion.36, bf16[8,8,64,128]{3,2,1,0:T(8,128)(2,1)S(1)} %bitcast.84, pred[8,8]{1,0:T(8,128)(4,1)S(1)} %get-tuple-element.277), kind=kOutput, calls=%fused_computation.5.clone.1 | convolution fusion | flops 403177472 | bytes 4194368 | tf_op jit(solution)/shard_map/while/body/eval_jaxpr/glpo,mglo,gl->mgp/dot_general | solution.py:59
  169.0 3.1 %fusion.37 = bf16[8,1,64,64]{3,1,2,0:T(2,128)(2,1)S(1)} fusion(f32[8,8,1,1]{1,2,3,0:T(1,128)S(1)} %copy.57, f32[64,8,8,64]{3,0,2,1:T(8,128)S(1)} %convolution_bitcast_fusion.2), kind=kOutput, calls=%fused_computation.3.clone.1 | convolution fusion | flops 3145728 | bytes 1114368 | tf_op jit(solution)/shard_map/while/body/eval_jaxpr/glpo,mglo,gl->mgp/dot_general | solution.py:59
  172.1 0.2 copy.59
  172.2 0.1 reshape.157
  172.4 0.1 reshape.156
  172.5 2.0 gather_fusion
  174.5 0.9 constant_dynamic-slice_fusion.2
  175.4 0.1 copy.58
  175.6 2.4 %fusion.36 = f32[8,8,128,64]{2,3,1,0:T(8,128)} fusion(f32[64,8,64,1]{0,2,3,1:T(8,128)S(1)} %bitcast.85, bf16[8,8,64,128]{3,2,1,0:T(8,128)(2,1)S(1)} %bitcast.83, pred[8,8]{1,0:T(8,128)(4,1)S(1)} %get-tuple-element.277), kind=kOutput, calls=%fused_computation.6.clone.1 | convolution fusion | flops 403177472 | bytes 3276864 | tf_op jit(solution)/shard_map/while/body/eval_jaxpr/mgp,mglo->glpo/dot_general | solution.py:58
  178.0 2.0 gather_fusion.1
  179.9 3.4 %convolution_bitcast_fusion.2 = f32[64,8,8,64]{3,0,2,1:T(8,128)S(1)} fusion(f32[8,8,128,64]{2,3,1,0:T(8,128)} %fusion.36, bf16[8,8,64,128]{3,2,1,0:T(8,128)(2,1)S(1)} %bitcast.84, pred[8,8]{1,0:T(8,128)(4,1)S(1)} %get-tuple-element.277), kind=kOutput, calls=%fused_computation.5.clone.1 | convolution fusion | flops 403177472 | bytes 4194368 | tf_op jit(solution)/shard_map/while/body/eval_jaxpr/glpo,mglo,gl->mgp/dot_general | solution.py:59
  183.5 3.1 %fusion.37 = bf16[8,1,64,64]{3,1,2,0:T(2,128)(2,1)S(1)} fusion(f32[8,8,1,1]{1,2,3,0:T(1,128)S(1)} %copy.57, f32[64,8,8,64]{3,0,2,1:T(8,128)S(1)} %convolution_bitcast_fusion.2), kind=kOutput, calls=%fused_computation.3.clone.1 | convolution fusion | flops 3145728 | bytes 1114368 | tf_op jit(solution)/shard_map/while/body/eval_jaxpr/glpo,mglo,gl->mgp/dot_general | solution.py:59
  186.6 0.2 copy.59
  186.8 0.1 reshape.157
  187.0 1.2 fusion.13
  188.2 0.5 copy.38
  188.8 32.7 %all_to_all.32 = f32[64,1,2048]{2,1,0:T(1,128)S(1)} all-to-all(f32[64,1,2048]{2,1,0:T(1,128)S(1)} %copy.38), channel_id=1, replica_groups=mesh['slab'=64,'obs'=8] {'slab'}, dimensions={0} | all-to-all | bytes 1048576 | tf_op jit(solution)/shard_map/all_to_all | solution.py:94
  221.4 0.8 copy.69
  (40 shorter events, 1.0 us)
Async XLA Ops:
  6.5 32.5 %all-to-all-start = ((f32[1,64,2048]{2,0,1:T(1,128)}), f32[1,64,2048]{2,0,1:T(1,128)S(1)}, u32[]{:S(2)}, u32[]{:S(2)}) async-start(f32[1,64,2048]{2,0,1:T(1,128)} %bitcast.93), calls=%async_computation | async-start | bytes 1048576 | tf_op jit(solution)/shard_map/all_to_all | solution.py:77
  21.4 60.4 %all-gather.3.cloned.1.call-start = ((), (), s32[]{:S(2)}) async-start(), calls=%async_computation.2 | async-start | bytes 2359296 | tf_op jit(solution)/shard_map/all_gather | solution.py:41
  39.1 0.8 copy-start
  40.1 4.3 %copy-start.2 = (f32[1,1024]{1,0:T(1,128)S(1)}, f32[1,1024]{1,0:T(1,128)}, u32[]{:S(2)}) copy-start(f32[1,1024]{1,0:T(1,128)} %param.15) | copy-start | bytes 12292
  40.1 4.3 %copy-start.1 = (f32[1,1024]{1,0:T(1,128)S(1)}, f32[1,1024]{1,0:T(1,128)}, u32[]{:S(2)}) copy-start(f32[1,1024]{1,0:T(1,128)} %param.14) | copy-start | bytes 12292
  40.1 6.7 %copy-start.3 = (s32[1,32,8]{1,2,0:T(8,128)S(1)}, s32[1,32,8]{1,2,0:T(8,128)}, u32[]{:S(2)}) copy-start(s32[1,32,8]{1,2,0:T(8,128)} %param.18) | copy-start | bytes 3076
  40.1 6.8 %copy-start.4 = (f32[1,32,8]{1,2,0:T(8,128)S(1)}, f32[1,32,8]{1,2,0:T(8,128)}, u32[]{:S(2)}) copy-start(f32[1,32,8]{1,2,0:T(8,128)} %param.19) | copy-start | bytes 3076
  46.1 79.9 %all-gather.5.cloned.1.call-start = ((), (), s32[]{:S(2)}) async-start(), calls=%async_computation.3 | async-start | bytes 2359296 | tf_op jit(solution)/shard_map/all_gather | solution.py:40
Sparse Core Ops, SparseCore 0:
  46.2 35.5 all-gather.2
  83.8 42.0 all-gather.4
where the time goes:
time: 230 us; the launch traced here: 229 us
  waiting for transfers between devices  90.7 us (39%)
  matrix products  35.7 us (16%)
  local copies, waits for them, and re-layouts  33.8 us (15%)
  blocking collectives  32.7 us (14%)
  starting transfers between devices  14.9 us (6%)
  between operations  14.2 us (6%)
  other arithmetic  6.66 us (3%)
    all_gather x1, waiting for transfers between devices, compute_increment(): lax.all_gather(prior_low, 'obs', axis=1, tiled=True)  41.5 us
    all_gather x1, waiting for transfers between devices, compute_increment(): lax.all_gather(gain_input, 'obs', axis=1, tiled=True)  33.9 us
    all_to_all x1, blocking collectives, local(): lax.all_to_all(analysis, 'slab', split_axis=0, concat_axis=1, tiled=True)  32.7 us
    dot_general x8, matrix products, one_group(): jnp.einsum('glpo,mglo,gl->mgp', covariance, picked_gain, scales, precisio...  26.2 us
    all_to_all x1, starting transfers between devices, local(): lax.all_to_all(background_members, 'slab', split_axis=1, concat_axis=0, t...  14.8 us
    all_to_all x1, waiting for transfers between devices, local(): lax.all_to_all(background_members, 'slab', split_axis=1, concat_axis=0, t...  14.5 us
    dot_general x4, matrix products, one_group(): jnp.einsum('mgp,mglo->glpo', local_dev, picked_prior, precision=highest)  9.56 us
    gather x4, local copies, waits for them, and re-layouts, one_group(): picked_prior = jnp.take(all_prior, chosen, axis=1).astype(jnp.float32)  7.9 us
  transfers between devices with their start and end apart: 3, of which 3 were waited for; matrix products, arithmetic and copies ran while one was open for 3% of the time, Pallas kernels for 0%

commit v1 on v0

--- a/solution.py
+++ b/solution.py
@@ -18,6 +18,11 @@
     coupling_listing,
     taper_factors,
 ):
+
+    def wires_link(x_in):
+        w1 = jnp.stack([x_in] * lax.axis_size("obs"))
+        return jnp.concatenate(lax.all_to_all(w1, "obs", 0, 0), axis=1)
+
     members = tile_work.shape[0]
     points = tile_work.shape[1]
     blocks = coupling_listing.shape[1]
@@ -36,10 +41,7 @@
     prior_low = prior_shift.astype(jnp.bfloat16)
     block_links = coupling_listing[0]
     factor = taper_factors[0] / (members - 1)
-    gathered = (
-        lax.all_gather(prior_low, "obs", axis=1, tiled=True),
-        lax.all_gather(gain_input, "obs", axis=1, tiled=True),
-    )
+    gathered = (wires_link(prior_low), lax.all_gather(gain_input, "obs", axis=1, tiled=True))
     all_prior = gathered[0].reshape(members, -1, OB)
     all_gain = gathered[1].reshape(members, -1, OB)
     group_size = math.gcd(blocks, 8)

time: 230 us -> 197 us (0.86)
  waiting for transfers between devices: 90.7 us -> 62.1 us
  blocking collectives: 32.7 us -> 25.3 us
  starting transfers between devices: 14.9 us -> 21.7 us
    all_gather x1 -> x0, waiting for transfers between devices: 41.5 us -> none  [compute_increment(): lax.all_gather(prior_low, 'obs', axis=1, tiled=True)]
    all_gather x1, waiting for transfers between devices: 33.9 us -> 47.6 us  [compute_increment(): lax.all_gather(gain_input, 'obs', axis=1, tiled=True)]
    all_to_all x1, blocking collectives: 32.7 us -> 25.3 us  [local(): lax.all_to_all(analysis, 'slab', split_axis=0, concat_axis=1, tiled=True)]
    all_to_all x0 -> x1, starting transfers between devices: none -> 6.82 us  [wires_link(): return jnp.concatenate(lax.all_to_all(w1, 'obs', 0, 0), axis=1)]
    dynamic_slice x8, local copies, waits for them, and re-layouts: 4.16 us -> 0.55 us  [one_group(): lax.dynamic_slice_in_dim(deviation, first_block * block_width, group_size...]
  transfers between devices with their start and end apart: 3 -> 3, of which waited for: 3 -> 2; matrix products, arithmetic and copies ran while one was open for 3% -> 3% of each run, Pallas kernels for 0% -> 0%
where the time goes in v1:
time: 197 us
  waiting for transfers between devices  62.1 us (32%)
  matrix products  35.7 us (18%)
  local copies, waits for them, and re-layouts  31.8 us (16%)
  blocking collectives  25.3 us (13%)
  starting transfers between devices  21.7 us (11%)
  between operations  14.2 us (7%)
  other arithmetic  5.32 us (3%)
    all_gather x1, waiting for transfers between devices, compute_increment(): lax.all_gather(gain_input, 'obs', axis=1, tiled=True)  47.6 us
    dot_general x8, matrix products, one_group(): jnp.einsum('glpo,mglo,gl->mgp', covariance, picked_gain, scales, precisio...  26.2 us
    all_to_all x1, blocking collectives, local(): lax.all_to_all(analysis, 'slab', split_axis=0, concat_axis=1, tiled=True)  25.3 us
    all_to_all x1, starting transfers between devices, local(): lax.all_to_all(background_members, 'slab', split_axis=1, concat_axis=0, t...  14.8 us
    all_to_all x1, waiting for transfers between devices, local(): lax.all_to_all(background_members, 'slab', split_axis=1, concat_axis=0, t...  14.5 us
    dot_general x4, matrix products, one_group(): jnp.einsum('mgp,mglo->glpo', local_dev, picked_prior, precision=highest)  9.54 us
    gather x4, local copies, waits for them, and re-layouts, one_group(): picked_prior = jnp.take(all_prior, chosen, axis=1).astype(jnp.float32)  8.2 us
    gather x4, local copies, waits for them, and re-layouts, one_group(): picked_gain = jnp.take(all_gain, chosen, axis=1).astype(jnp.float32)  7.89 us
  transfers between devices with their start and end apart: 3, of which 2 were waited for; matrix products, arithmetic and copies ran while one was open for 3% of the time, Pallas kernels for 0%

profile of v1, /device:TPU:1, one launch (start us, length us, event | category | flops | bytes accessed | tf_op | source)
XLA Modules:
  0.0 196.6 jit_solution(2773102462150293254)
XLA Ops:
  6.5 14.8 %all-to-all-start = ((f32[1,64,2048]{2,0,1:T(1,128)}), f32[1,64,2048]{2,0,1:T(1,128)S(1)}, u32[]{:S(2)}, u32[]{:S(2)}) async-start(f32[1,64,2048]{2,0,1:T(1,128)} %bitcast.93), calls=%async_computation | async-start | bytes 1048576 | tf_op jit(solution)/shard_map/all_to_all | solution.py:79
  22.1 1.1 copy.43
  23.1 0.7 iota_compare_fusion
  23.8 0.7 compare_select_fusion.1
  24.5 14.5 %all-to-all-done = f32[1,64,2048]{2,0,1:T(1,128)S(1)} async-done(((f32[1,64,2048]{2,0,1:T(1,128)}), f32[1,64,2048]{2,0,1:T(1,128)S(1)}, u32[]{:S(2)}, u32[]{:S(2)}) %all-to-all-start) | async-done | bytes 524320 | tf_op jit(solution)/shard_map/all_to_all | solution.py:79
  39.1 0.2 copy.63
  39.2 0.6 copy-done
  39.9 0.2 copy.44
  40.1 2.8 %gather_fusion.2 = f32[1024,64]{1,0:T(8,128)S(1)} fusion(f32[64,2048]{0,1:T(8,128)S(1)} %copy.44, s32[1024]{0:T(1024)S(1)} %broadcast_clamp_fusion), kind=kCustom, calls=%fused_computation.2 | custom fusion | bytes 528384 | tf_op jit(solution)/shard_map/jit(_take)/gather | solution.py:33
  42.9 0.4 select_reduce_fusion
  43.3 0.5 fusion.18
  43.8 1.6 fusion.17
  45.5 0.1 copy.45
  45.6 1.1 stack.2
  46.7 6.8 %all-to-all-start.1 = ((bf16[8,64,1024]{2,1,0:T(8,128)(2,1)}), bf16[8,64,1024]{2,1,0:T(8,128)(2,1)S(1)}, u32[]{:S(2)}, u32[]{:S(2)}) async-start(bf16[8,64,1024]{2,1,0:T(8,128)(2,1)} %stack.2), calls=%async_computation.1 | async-start | bytes 2097152 | tf_op jit(solution)/shard_map/all_to_all | solution.py:24
  53.6 0.1 copy.42
  53.8 47.6 %all-gather.2.cloned.1.call-done = bf16[64,8192]{0,1:T(8,128)(2,1)} async-done(((bf16[64,1024]{0,1:T(8,128)(2,1)}), bf16[64,8192]{0,1:T(8,128)(2,1)}) %all-gather.2.cloned.1.call-update) | async-done | bytes 1048592 | tf_op jit(solution)/shard_map/all_gather | solution.py:44
  101.3 2.7 %copy.47 = bf16[64,64,128]{2,0,1:T(8,128)(2,1)} copy(bf16[64,64,128]{0,2,1:T(8,128)(2,1)} %bitcast.91) | data formatting | bytes 2097152 | tf_op jit(solution)/shard_map/while | solution.py:65
  104.0 0.6 copy.46
  104.6 0.5 reshape_reshape.3
  105.1 1.7 copy.48
  106.8 55.1 %while.15 = (s32[]{:T(128)}, bf16[64,2048]{1,0:T(8,128)(2,1)S(1)}, s32[32,8]{1,0:T(8,128)S(1)}, bf16[64,64,128]{2,0,1:T(8,128)(2,1)}, bf16[64,64,128]{2,0,1:T(8,...) while((s32[]{:T(128)}, bf16[64,2048]{1,0:T(8,128)(2,1)S(1)}, ...), condition=%wide.region_4.6_spmd, body=%wide.region_3.5_spmd.sunk | while | flops 809502080 | bytes 17898976 | solution.py:65
  106.8 0.1 reshape.176
  106.9 2.0 %gather_fusion = bf16[64,64,128]{2,1,0:T(8,128)(2,1)S(1)} fusion(bf16[64,64,128]{2,0,1:T(8,128)(2,1)} %get-tuple-element.315, s32[1024]{0:T(1024)S(1)} %pad_clamp_fusion.2), kind=kCustom, calls=%fused_computation.1.clone.clone.1 | custom fusion | bytes 2097408 | tf_op jit(solution)/shard_map/while/body/eval_jaxpr/jit(_take)/gather | solution.py:58
  109.0 0.1 copy.70
  109.1 2.4 %fusion.36 = f32[8,8,128,64]{2,3,1,0:T(8,128)} fusion(f32[64,8,64,1]{0,2,3,1:T(8,128)S(1)} %bitcast.85, bf16[8,8,64,128]{3,2,1,0:T(8,128)(2,1)S(1)} %bitcast.83, pred[8,8]{1,0:T(8,128)(4,1)S(1)} %get-tuple-element.284), kind=kOutput, calls=%fused_computation.6.clone.1 | convolution fusion | flops 403177472 | bytes 3276864 | tf_op jit(solution)/shard_map/while/body/eval_jaxpr/mgp,mglo->glpo/dot_general | solution.py:60
  111.5 2.0 %gather_fusion.1 = bf16[64,64,128]{2,1,0:T(8,128)(2,1)S(1)} fusion(bf16[64,64,128]{2,0,1:T(8,128)(2,1)} %get-tuple-element.314, s32[1024]{0:T(1024)S(1)} %pad_clamp_fusion.2), kind=kCustom, calls=%fused_computation.clone.clone.1 | custom fusion | bytes 2097408 | tf_op jit(solution)/shard_map/while/body/eval_jaxpr/jit(_take)/gather | solution.py:59
  113.5 3.4 %convolution_bitcast_fusion.2 = f32[64,8,8,64]{3,0,2,1:T(8,128)S(1)} fusion(f32[8,8,128,64]{2,3,1,0:T(8,128)} %fusion.36, bf16[8,8,64,128]{3,2,1,0:T(8,128)(2,1)S(1)} %bitcast.84, pred[8,8]{1,0:T(8,128)(4,1)S(1)} %get-tuple-element.284), kind=kOutput, calls=%fused_computation.5.clone.1 | convolution fusion | flops 403177472 | bytes 4194368 | tf_op jit(solution)/shard_map/while/body/eval_jaxpr/glpo,mglo,gl->mgp/dot_general | solution.py:61
  117.0 0.1 dynamic-slice_bitcast_fusion.2
  117.1 3.1 %fusion.37 = bf16[8,1,64,64]{3,1,2,0:T(2,128)(2,1)S(1)} fusion(f32[8,8,1,1]{1,2,3,0:T(1,128)S(1)} %copy.69, f32[64,8,8,64]{3,0,2,1:T(8,128)S(1)} %convolution_bitcast_fusion.2), kind=kOutput, calls=%fused_computation.3.clone.1 | convolution fusion | flops 3145728 | bytes 1114368 | tf_op jit(solution)/shard_map/while/body/eval_jaxpr/glpo,mglo,gl->mgp/dot_general | solution.py:61
  120.2 0.2 copy.71
  120.4 0.1 reshape.177
  120.6 0.1 reshape.176
  120.7 2.0 %gather_fusion = bf16[64,64,128]{2,1,0:T(8,128)(2,1)S(1)} fusion(bf16[64,64,128]{2,0,1:T(8,128)(2,1)} %get-tuple-element.315, s32[1024]{0:T(1024)S(1)} %pad_clamp_fusion.2), kind=kCustom, calls=%fused_computation.1.clone.clone.1 | custom fusion | bytes 2097408 | tf_op jit(solution)/shard_map/while/body/eval_jaxpr/jit(_take)/gather | solution.py:58
  122.8 0.1 copy.70
  122.9 2.4 %fusion.36 = f32[8,8,128,64]{2,3,1,0:T(8,128)} fusion(f32[64,8,64,1]{0,2,3,1:T(8,128)S(1)} %bitcast.85, bf16[8,8,64,128]{3,2,1,0:T(8,128)(2,1)S(1)} %bitcast.83, pred[8,8]{1,0:T(8,128)(4,1)S(1)} %get-tuple-element.284), kind=kOutput, calls=%fused_computation.6.clone.1 | convolution fusion | flops 403177472 | bytes 3276864 | tf_op jit(solution)/shard_map/while/body/eval_jaxpr/mgp,mglo->glpo/dot_general | solution.py:60
  125.3 2.0 %gather_fusion.1 = bf16[64,64,128]{2,1,0:T(8,128)(2,1)S(1)} fusion(bf16[64,64,128]{2,0,1:T(8,128)(2,1)} %get-tuple-element.314, s32[1024]{0:T(1024)S(1)} %pad_clamp_fusion.2), kind=kCustom, calls=%fused_computation.clone.clone.1 | custom fusion | bytes 2097408 | tf_op jit(solution)/shard_map/while/body/eval_jaxpr/jit(_take)/gather | solution.py:59
  127.3 3.4 %convolution_bitcast_fusion.2 = f32[64,8,8,64]{3,0,2,1:T(8,128)S(1)} fusion(f32[8,8,128,64]{2,3,1,0:T(8,128)} %fusion.36, bf16[8,8,64,128]{3,2,1,0:T(8,128)(2,1)S(1)} %bitcast.84, pred[8,8]{1,0:T(8,128)(4,1)S(1)} %get-tuple-element.284), kind=kOutput, calls=%fused_computation.5.clone.1 | convolution fusion | flops 403177472 | bytes 4194368 | tf_op jit(solution)/shard_map/while/body/eval_jaxpr/glpo,mglo,gl->mgp/dot_general | solution.py:61
  130.8 0.1 dynamic-slice_bitcast_fusion.2
  130.9 3.1 %fusion.37 = bf16[8,1,64,64]{3,1,2,0:T(2,128)(2,1)S(1)} fusion(f32[8,8,1,1]{1,2,3,0:T(1,128)S(1)} %copy.69, f32[64,8,8,64]{3,0,2,1:T(8,128)S(1)} %convolution_bitcast_fusion.2), kind=kOutput, calls=%fused_computation.3.clone.1 | convolution fusion | flops 3145728 | bytes 1114368 | tf_op jit(solution)/shard_map/while/body/eval_jaxpr/glpo,mglo,gl->mgp/dot_general | solution.py:61
  134.0 0.2 copy.71
  134.2 0.1 reshape.177
  134.4 0.1 reshape.176
  134.5 2.0 %gather_fusion = bf16[64,64,128]{2,1,0:T(8,128)(2,1)S(1)} fusion(bf16[64,64,128]{2,0,1:T(8,128)(2,1)} %get-tuple-element.315, s32[1024]{0:T(1024)S(1)} %pad_clamp_fusion.2), kind=kCustom, calls=%fused_computation.1.clone.clone.1 | custom fusion | bytes 2097408 | tf_op jit(solution)/shard_map/while/body/eval_jaxpr/jit(_take)/gather | solution.py:58
  136.6 0.1 copy.70
  136.7 2.4 %fusion.36 = f32[8,8,128,64]{2,3,1,0:T(8,128)} fusion(f32[64,8,64,1]{0,2,3,1:T(8,128)S(1)} %bitcast.85, bf16[8,8,64,128]{3,2,1,0:T(8,128)(2,1)S(1)} %bitcast.83, pred[8,8]{1,0:T(8,128)(4,1)S(1)} %get-tuple-element.284), kind=kOutput, calls=%fused_computation.6.clone.1 | convolution fusion | flops 403177472 | bytes 3276864 | tf_op jit(solution)/shard_map/while/body/eval_jaxpr/mgp,mglo->glpo/dot_general | solution.py:60
  139.1 2.0 %gather_fusion.1 = bf16[64,64,128]{2,1,0:T(8,128)(2,1)S(1)} fusion(bf16[64,64,128]{2,0,1:T(8,128)(2,1)} %get-tuple-element.314, s32[1024]{0:T(1024)S(1)} %pad_clamp_fusion.2), kind=kCustom, calls=%fused_computation.clone.clone.1 | custom fusion | bytes 2097408 | tf_op jit(solution)/shard_map/while/body/eval_jaxpr/jit(_take)/gather | solution.py:59
  141.1 3.4 %convolution_bitcast_fusion.2 = f32[64,8,8,64]{3,0,2,1:T(8,128)S(1)} fusion(f32[8,8,128,64]{2,3,1,0:T(8,128)} %fusion.36, bf16[8,8,64,128]{3,2,1,0:T(8,128)(2,1)S(1)} %bitcast.84, pred[8,8]{1,0:T(8,128)(4,1)S(1)} %get-tuple-element.284), kind=kOutput, calls=%fused_computation.5.clone.1 | convolution fusion | flops 403177472 | bytes 4194368 | tf_op jit(solution)/shard_map/while/body/eval_jaxpr/glpo,mglo,gl->mgp/dot_general | solution.py:61
  144.7 3.1 %fusion.37 = bf16[8,1,64,64]{3,1,2,0:T(2,128)(2,1)S(1)} fusion(f32[8,8,1,1]{1,2,3,0:T(1,128)S(1)} %copy.69, f32[64,8,8,64]{3,0,2,1:T(8,128)S(1)} %convolution_bitcast_fusion.2), kind=kOutput, calls=%fused_computation.3.clone.1 | convolution fusion | flops 3145728 | bytes 1114368 | tf_op jit(solution)/shard_map/while/body/eval_jaxpr/glpo,mglo,gl->mgp/dot_general | solution.py:61
  147.8 0.2 copy.71
  147.9 0.1 reshape.177
  148.2 0.1 reshape.176
  148.3 2.0 %gather_fusion = bf16[64,64,128]{2,1,0:T(8,128)(2,1)S(1)} fusion(bf16[64,64,128]{2,0,1:T(8,128)(2,1)} %get-tuple-element.315, s32[1024]{0:T(1024)S(1)} %pad_clamp_fusion.2), kind=kCustom, calls=%fused_computation.1.clone.clone.1 | custom fusion | bytes 2097408 | tf_op jit(solution)/shard_map/while/body/eval_jaxpr/jit(_take)/gather | solution.py:58
  150.4 0.1 copy.70
  150.5 2.4 %fusion.36 = f32[8,8,128,64]{2,3,1,0:T(8,128)} fusion(f32[64,8,64,1]{0,2,3,1:T(8,128)S(1)} %bitcast.85, bf16[8,8,64,128]{3,2,1,0:T(8,128)(2,1)S(1)} %bitcast.83, pred[8,8]{1,0:T(8,128)(4,1)S(1)} %get-tuple-element.284), kind=kOutput, calls=%fused_computation.6.clone.1 | convolution fusion | flops 403177472 | bytes 3276864 | tf_op jit(solution)/shard_map/while/body/eval_jaxpr/mgp,mglo->glpo/dot_general | solution.py:60
  152.9 2.0 %gather_fusion.1 = bf16[64,64,128]{2,1,0:T(8,128)(2,1)S(1)} fusion(bf16[64,64,128]{2,0,1:T(8,128)(2,1)} %get-tuple-element.314, s32[1024]{0:T(1024)S(1)} %pad_clamp_fusion.2), kind=kCustom, calls=%fused_computation.clone.clone.1 | custom fusion | bytes 2097408 | tf_op jit(solution)/shard_map/while/body/eval_jaxpr/jit(_take)/gather | solution.py:59
  154.8 3.4 %convolution_bitcast_fusion.2 = f32[64,8,8,64]{3,0,2,1:T(8,128)S(1)} fusion(f32[8,8,128,64]{2,3,1,0:T(8,128)} %fusion.36, bf16[8,8,64,128]{3,2,1,0:T(8,128)(2,1)S(1)} %bitcast.84, pred[8,8]{1,0:T(8,128)(4,1)S(1)} %get-tuple-element.284), kind=kOutput, calls=%fused_computation.5.clone.1 | convolution fusion | flops 403177472 | bytes 4194368 | tf_op jit(solution)/shard_map/while/body/eval_jaxpr/glpo,mglo,gl->mgp/dot_general | solution.py:61
  158.5 3.1 %fusion.37 = bf16[8,1,64,64]{3,1,2,0:T(2,128)(2,1)S(1)} fusion(f32[8,8,1,1]{1,2,3,0:T(1,128)S(1)} %copy.69, f32[64,8,8,64]{3,0,2,1:T(8,128)S(1)} %convolution_bitcast_fusion.2), kind=kOutput, calls=%fused_computation.3.clone.1 | convolution fusion | flops 3145728 | bytes 1114368 | tf_op jit(solution)/shard_map/while/body/eval_jaxpr/glpo,mglo,gl->mgp/dot_general | solution.py:61
  161.6 0.2 copy.71
  161.7 0.1 reshape.177
  161.9 1.2 fusion.13
  163.1 0.5 copy.50
  163.7 25.3 %all_to_all.37 = f32[64,1,2048]{2,1,0:T(1,128)S(1)} all-to-all(f32[64,1,2048]{2,1,0:T(1,128)S(1)} %copy.50), channel_id=1, replica_groups=mesh['slab'=64,'obs'=8] {'slab'}, dimensions={0} | all-to-all | bytes 1048576 | tf_op jit(solution)/shard_map/all_to_all | solution.py:96
  189.0 0.8 copy.81
  (59 shorter events, 0.9 us)
Async XLA Ops:
  6.5 32.5 %all-to-all-start = ((f32[1,64,2048]{2,0,1:T(1,128)}), f32[1,64,2048]{2,0,1:T(1,128)S(1)}, u32[]{:S(2)}, u32[]{:S(2)}) async-start(f32[1,64,2048]{2,0,1:T(1,128)} %bitcast.93), calls=%async_computation | async-start | bytes 1048576 | tf_op jit(solution)/shard_map/all_to_all | solution.py:79
  21.4 80.0 %all-gather.2.cloned.1.call-start = ((), (), s32[]{:S(2)}) async-start(), calls=%async_computation.3 | async-start | bytes 2359296 | tf_op jit(solution)/shard_map/all_gather | solution.py:44
  39.1 0.8 copy-start
  40.1 3.7 %copy-start.4 = (f32[1,1024]{1,0:T(1,128)S(1)}, f32[1,1024]{1,0:T(1,128)}, u32[]{:S(2)}) copy-start(f32[1,1024]{1,0:T(1,128)} %param.15) | copy-start | bytes 12292
  40.1 3.7 %copy-start.3 = (f32[1,1024]{1,0:T(1,128)S(1)}, f32[1,1024]{1,0:T(1,128)}, u32[]{:S(2)}) copy-start(f32[1,1024]{1,0:T(1,128)} %param.14) | copy-start | bytes 12292
  45.5 8.1 %copy-start.5 = (s32[1,32,8]{1,2,0:T(8,128)S(1)}, s32[1,32,8]{1,2,0:T(8,128)}, u32[]{:S(2)}) copy-start(s32[1,32,8]{1,2,0:T(8,128)} %param.18) | copy-start | bytes 3076
  45.5 8.2 %copy-start.6 = (f32[1,32,8]{1,2,0:T(8,128)S(1)}, f32[1,32,8]{1,2,0:T(8,128)}, u32[]{:S(2)}) copy-start(f32[1,32,8]{1,2,0:T(8,128)} %param.19) | copy-start | bytes 3076
  46.7 57.3 %all-to-all-start.1 = ((bf16[8,64,1024]{2,1,0:T(8,128)(2,1)}), bf16[8,64,1024]{2,1,0:T(8,128)(2,1)S(1)}, u32[]{:S(2)}, u32[]{:S(2)}) async-start(bf16[8,64,1024]{2,1,0:T(8,128)(2,1)} %stack.2), calls=%async_computation.1 | async-start | bytes 2097152 | tf_op jit(solution)/shard_map/all_to_all | solution.py:24
  106.8 4.7 %copy-start.1 = (f32[64,2048]{1,0:T(8,128)}, f32[64,2048]{1,0:T(8,128)S(1)}, u32[]{:S(2)}) copy-start(f32[64,2048]{1,0:T(8,128)S(1)} %get-tuple-element.316) | copy-start | bytes 1572868 | tf_op jit(solution)/shard_map/while
  117.0 3.6 %copy-start.2 = (f32[64,2048]{1,0:T(8,128)S(1)}, f32[64,2048]{1,0:T(8,128)}, u32[]{:S(2)}) copy-start(f32[64,2048]{1,0:T(8,128)} %copy-done.1) | copy-start | bytes 1572868 | tf_op jit(solution)/shard_map/while
  120.6 4.7 %copy-start.1 = (f32[64,2048]{1,0:T(8,128)}, f32[64,2048]{1,0:T(8,128)S(1)}, u32[]{:S(2)}) copy-start(f32[64,2048]{1,0:T(8,128)S(1)} %get-tuple-element.316) | copy-start | bytes 1572868 | tf_op jit(solution)/shard_map/while
  130.7 3.6 %copy-start.2 = (f32[64,2048]{1,0:T(8,128)S(1)}, f32[64,2048]{1,0:T(8,128)}, u32[]{:S(2)}) copy-start(f32[64,2048]{1,0:T(8,128)} %copy-done.1) | copy-start | bytes 1572868 | tf_op jit(solution)/shard_map/while
  134.4 4.7 %copy-start.1 = (f32[64,2048]{1,0:T(8,128)}, f32[64,2048]{1,0:T(8,128)S(1)}, u32[]{:S(2)}) copy-start(f32[64,2048]{1,0:T(8,128)S(1)} %get-tuple-element.316) | copy-start | bytes 1572868 | tf_op jit(solution)/shard_map/while
  144.5 3.6 %copy-start.2 = (f32[64,2048]{1,0:T(8,128)S(1)}, f32[64,2048]{1,0:T(8,128)}, u32[]{:S(2)}) copy-start(f32[64,2048]{1,0:T(8,128)} %copy-done.1) | copy-start | bytes 1572868 | tf_op jit(solution)/shard_map/while
  148.1 4.7 %copy-start.1 = (f32[64,2048]{1,0:T(8,128)}, f32[64,2048]{1,0:T(8,128)S(1)}, u32[]{:S(2)}) copy-start(f32[64,2048]{1,0:T(8,128)S(1)} %get-tuple-element.316) | copy-start | bytes 1572868 | tf_op jit(solution)/shard_map/while
  158.3 3.6 %copy-start.2 = (f32[64,2048]{1,0:T(8,128)S(1)}, f32[64,2048]{1,0:T(8,128)}, u32[]{:S(2)}) copy-start(f32[64,2048]{1,0:T(8,128)} %copy-done.1) | copy-start | bytes 1572868 | tf_op jit(solution)/shard_map/while
Sparse Core Ops, SparseCore 0:
  45.6 55.6 all-gather.1
